TPU v7x, 32 devices: a whole 2x2x4 slice. The times are simulated.
32 devices in a mesh: mix: 2 (over x), seq: 16 (over z, y, core).
Axes of the slice: x: 2, y: 2, z: 4, core: 2. Of those that a mesh axis runs over, the one named last changes fastest.
Arguments:
- frames: bfloat16 [4096, 1024], P(('mix', 'seq')), parts along dimension 0, may hold values from -18 to 18
- segment_ids: int32 [4096], P(('mix', 'seq')), parts along dimension 0, may hold values from 0 to 2, never falling along the last dimension, each value on 1 to 1500 neighbouring positions
- out_grad: bfloat16 [4096, 1024], P(('mix', 'seq')), parts along dimension 0, may hold values from -6 to 6
- ln_gain: float32 [2048], P(('mix', 'seq')), parts along dimension 0, may hold values from 0.5 to 2
- w_in: bfloat16 [2048, 2048], P(('mix', 'seq')), parts along dimension 0, may hold values from -0.1875 to 0.1875
- dw_kernel: float32 [62, 1024], P('mix', 'seq'), parts along dimension 0, may hold values from -1 to 1
- bn_gain: float32 [2048], P(('mix', 'seq')), parts along dimension 0, may hold values from 0.5 to 2
- bn_bias: float32 [2048], P(('mix', 'seq')), parts along dimension 0, may hold values from -3 to 3
- w_out: bfloat16 [2048, 1024], P(('mix', 'seq')), parts along dimension 0, may hold values from -0.1875 to 0.1875
Outputs:
- outputs: bfloat16 [4096, 1024], P(('mix', 'seq')), parts along dimension 0
- grad_frames: bfloat16 [4096, 1024], P(('mix', 'seq')), parts along dimension 0
- grad_w_in: float32 [2048, 2048], P(('mix', 'seq')), parts along dimension 0
- grad_w_out: float32 [2048, 1024], P(('mix', 'seq')), parts along dimension 0
- grad_kernel: float32 [62, 1024], P('mix', 'seq'), parts along dimension 0
- grad_ln_gain: float32 [2048], P(('mix', 'seq')), parts along dimension 0
- grad_bn_gain: float32 [2048], P(('mix', 'seq')), parts along dimension 0
- grad_bn_bias: float32 [2048], P(('mix', 'seq')), parts along dimension 0
There are 2 independent parts, one for each index of `mix`. A program takes and returns all parts, laid end to end along the dimension named above; each array names one. Nothing has to cross between parts.
Inputs may be any that keep to these rules, and one draw needn't show every extreme that they name: `segment_ids`: ids never fall along the stream; every utterance number is used, by 1 to 1500 consecutive frames, one utterance exactly 1500.
All inputs are finite; a program needn't handle non-finite values.
Results may differ from a plain program's by a relative error of at most 0.012.
The roundings to bfloat16 on the way count: a program that leaves them out, or rounds other values in their place, can miss the bound.
Values may be sent and summed in bfloat16 or wider, within the bound.
No kernel may reach another device: no remote copies, remote signals or barrier semaphores. Data moves between devices by JAX's collectives and lax.ppermute only.
A program may use at most 128 MiB of HBM per device.

v0:
```python
import math
import jax
import jax.numpy as jnp
from jax import lax
from jax.sharding import PartitionSpec as P

EPSILON = 1e-05


def with_halo(cells, sides, width):
    for axis, dim in sides:
        count = lax.axis_size(axis)
        ends = count - 1
        head = lax.slice_in_dim(cells, 0, width, axis=dim)
        tail = lax.slice_in_dim(cells, cells.shape[dim] - width, cells.shape[dim], axis=dim)
        cells = jnp.concatenate(
            [
                lax.ppermute(tail, axis, [(i, (i + 1) % count) for i in range(ends)]),
                cells,
                lax.ppermute(head, axis, [((i + 1) % count, i) for i in range(ends)]),
            ],
            axis=dim,
        )
    return cells


def local(frames, segment_ids, out_grad, ln_gain, w_in, dw_kernel, bn_gain, bn_bias, w_out):
    frame_count = frames.shape[0]
    width = frames.shape[1]
    taps = dw_kernel.shape[0]
    margin = taps // 2
    devices = lax.axis_size("seq")
    stream = frame_count * devices
    grad_scale = 1.0 / math.sqrt(stream)
    share = width // devices
    gains, kernel, bn_scale, bn_shift = (
        lax.all_gather(ln_gain, "seq", axis=0, tiled=True),
        lax.all_gather(dw_kernel, "seq", axis=1, tiled=True),
        lax.all_gather(bn_gain, "seq", axis=0, tiled=True),
        lax.all_gather(bn_bias, "seq", axis=0, tiled=True),
    )
    own_ids = segment_ids + 1
    padded_ids = with_halo(own_ids, (("seq", 0),), margin)
    masks = [
        (padded_ids[tap_index : tap_index + frame_count] == own_ids).astype(jnp.float32)[:, None]
        for tap_index in range(taps)
    ]
    frames_float = frames.astype(jnp.float32)
    mean_ln = jnp.mean(frames_float, axis=1, keepdims=True)
    centred = frames_float - mean_ln
    rstd_ln = lax.rsqrt(jnp.mean(centred * centred, axis=1, keepdims=True) + EPSILON)
    ln_hat = centred * rstd_ln
    ln_x = (ln_hat * gains).astype(jnp.bfloat16)
    columns = ln_x
    hidden = jnp.dot(
        columns, lax.all_gather(w_in, "seq", axis=0, tiled=True), preferred_element_type=jnp.float32
    )
    left_half = hidden[:, :width]
    right_gate = jax.nn.sigmoid(hidden[:, width:])
    glu = (left_half * right_gate).astype(jnp.bfloat16)
    padded_glu = with_halo(glu, (("seq", 0),), margin)
    conv_out = jnp.zeros((frame_count, width), jnp.float32)
    for tap_index in range(taps):
        conv_out = (
            conv_out
            + kernel[tap_index]
            * padded_glu[tap_index : tap_index + frame_count].astype(jnp.float32)
            * masks[tap_index]
        )
    plain_sums, square_sums = lax.psum(
        (jnp.sum(conv_out, axis=0), jnp.sum(conv_out * conv_out, axis=0)), "seq"
    )
    bn_mean = plain_sums / stream
    bn_var = square_sums / stream - bn_mean * bn_mean
    bn_rstd = lax.rsqrt(bn_var + EPSILON)
    bn_hat = (conv_out - bn_mean) * bn_rstd
    zed = bn_hat * bn_scale + bn_shift
    zed_gate = jax.nn.sigmoid(zed)
    activation = (zed * zed_gate).astype(jnp.bfloat16)
    columns = activation
    projected = jnp.dot(
        columns,
        lax.all_gather(w_out, "seq", axis=0, tiled=True),
        preferred_element_type=jnp.float32,
    )
    outputs = (frames_float + projected).astype(jnp.bfloat16)
    grad_w_out = lax.psum_scatter(
        jnp.einsum("fa,fb->ab", activation, out_grad, preferred_element_type=jnp.float32)
        * grad_scale,
        "seq",
        scatter_dimension=0,
        tiled=True,
    )
    grad_act = jnp.einsum(
        "fe,ne->fn",
        out_grad,
        lax.all_gather(w_out, "seq", axis=0, tiled=True),
        preferred_element_type=jnp.float32,
    )
    grad_zed = grad_act * zed_gate * (1.0 + zed * (1.0 - zed_gate))
    bias_total, gain_total = lax.psum(
        (jnp.sum(grad_zed, axis=0), jnp.sum(grad_zed * bn_hat, axis=0)), "seq"
    )
    grad_conv = bn_scale * bn_rstd * (grad_zed - bias_total / stream - bn_hat * gain_total / stream)
    first_channel = lax.axis_index("seq") * share
    grad_bn_bias = lax.dynamic_slice_in_dim(bias_total, first_channel, share, 0) * grad_scale
    grad_bn_gain = lax.dynamic_slice_in_dim(gain_total, first_channel, share, 0) * grad_scale
    kernel_rows = [
        jnp.sum(
            grad_conv
            * padded_glu[tap_index : tap_index + frame_count].astype(jnp.float32)
            * masks[tap_index],
            axis=0,
        )
        for tap_index in range(taps)
    ]
    kernel_term = jnp.stack(kernel_rows) * grad_scale
    padded_conv = with_halo(grad_conv, (("seq", 0),), margin)
    grad_glu = jnp.zeros((frame_count, width), jnp.float32)
    for tap_index in range(taps):
        mirror = 2 * margin - tap_index
        grad_glu = (
            grad_glu
            + kernel[tap_index] * padded_conv[mirror : mirror + frame_count] * masks[mirror]
        )
    grad_hidden = jnp.concatenate(
        [grad_glu * right_gate, grad_glu * left_half * right_gate * (1.0 - right_gate)], axis=1
    ).astype(jnp.bfloat16)
    grad_ln = jnp.einsum(
        "fe,ne->fn",
        grad_hidden,
        lax.all_gather(w_in, "seq", axis=0, tiled=True),
        preferred_element_type=jnp.float32,
    )
    in_term = (
        jnp.einsum("fa,fb->ab", ln_x, grad_hidden, preferred_element_type=jnp.float32) * grad_scale
    )
    gain_term = jnp.sum(grad_ln * ln_hat, axis=0) * grad_scale
    grad_w_in, grad_kernel, grad_ln_gain = (
        lax.psum_scatter(in_term, "seq", scatter_dimension=0, tiled=True),
        lax.psum_scatter(kernel_term, "seq", scatter_dimension=1, tiled=True),
        lax.psum_scatter(gain_term, "seq", scatter_dimension=0, tiled=True),
    )
    grad_hat = grad_ln * gains
    grad_input = rstd_ln * (
        grad_hat
        - jnp.mean(grad_hat, axis=1, keepdims=True)
        - ln_hat * jnp.mean(grad_hat * ln_hat, axis=1, keepdims=True)
    )
    grad_frames = (out_grad.astype(jnp.float32) + grad_input).astype(jnp.bfloat16)
    return (
        outputs,
        grad_frames,
        grad_w_in,
        grad_w_out,
        grad_kernel,
        grad_ln_gain,
        grad_bn_gain,
        grad_bn_bias,
    )


def solution(mesh):
    return jax.shard_map(
        local,
        mesh=mesh,
        in_specs=(
            P(("mix", "seq"), None),
            P(("mix", "seq")),
            P(("mix", "seq"), None),
            P(("mix", "seq")),
            P(("mix", "seq"), None),
            P("mix", "seq"),
            P(("mix", "seq")),
            P(("mix", "seq")),
            P(("mix", "seq"), None),
        ),
        out_specs=(
            P(("mix", "seq"), None),
            P(("mix", "seq"), None),
            P(("mix", "seq"), None),
            P(("mix", "seq"), None),
            P("mix", "seq"),
            P(("mix", "seq")),
            P(("mix", "seq")),
            P(("mix", "seq")),
        ),
        check_vma=False,
    )
```

profile of v0, /device:TPU:0, one launch (start us, length us, event | category | flops | bytes accessed | tf_op | source)
XLA Modules:
  0.0 432.6 jit_solution(1981038902537433708)
XLA Ops:
  7.2 0.0 all-gather.4.cloned.1.call-start
  7.2 0.7 all-gather.4.cloned.1.call-update
  7.9 0.0 all-gather.6.cloned.1.call-start
  7.9 0.7 all-gather.6.cloned.1.call-update
  8.6 0.0 reduce-scatter.10.cloned.1.call-start
  8.7 0.7 broadcast_add_fusion
  9.4 0.1 fusion.302
  9.4 2.3 collective-permute-start.1
  11.8 1.3 collective-permute-start.3
  13.1 26.5 %all-gather = f32[16,64,31]{1,2,0:T(8,128)S(1)} all-gather(f32[1,64,31]{1,2,0:T(8,128)} %bitcast.175), channel_id=1, replica_groups=mesh['mix'=2,'seq'=16] {'seq'}, dimensions={0}, use_global_device_ids=true | all-gather | bytes 134912 | tf_op jit(solution)/shard_map/all_gather | solution.py:38
  39.6 0.2 copy.18
  39.7 0.0 copy-start.3
  39.7 0.1 reshape.84
  39.9 1.3 fusion.301
  41.9 0.9 dynamic-update-slice.2
  42.7 0.8 dynamic-update-slice
  43.6 30.2 %all-reduce = f32[1024]{0:T(1024)S(1)} all-reduce(f32[1024]{0:T(1024)S(1)} %dynamic-update-slice), channel_id=1, replica_groups=mesh['mix'=2,'seq'=16] {'seq'}, use_global_device_ids=true, to_apply=%add | all-reduce | flops 1024 | bytes 8192
  73.8 1.1 convert_reduce_fusion
  74.9 1.2 fusion.129
  76.1 0.0 copy-start.2
  76.1 0.1 fusion.299
  76.2 0.9 dynamic-update-slice.1
  77.1 0.1 pad_add_fusion
  77.1 0.7 compare_convert_fusion.29
  77.9 0.0 all-gather.4.cloned.1.call-done
  77.9 3.1 fusion.291
  81.0 0.1 multiply_convert_fusion.3
  81.2 1.5 collective-permute-start
  82.7 1.3 collective-permute-start.2
  84.0 0.1 compare_convert_fusion.14
  84.1 1.7 collective-permute-done.2
  85.8 4.7 %fusion.294 = (f32[1024]{0:T(1024)S(1)}, f32[1024]{0:T(1024)S(1)}, f32[128,1024]{1,0:T(8,128)S(1)}) fusion(f32[128]{0:T(128)S(1)} %get-tuple-element.110, bf16[15,1024]{1,0:T(8,128)(2,1)S(1)} %collective-permute-done.2, bf16[128,1024]{1,0:T(8,128)(2,1)S(1)} %multiply_convert_fusion.3, f32[1024]{0:T(1024)S(1)} %bitcast.107, f32[128]{0:T(128)S(1)} %get-tuple-element.111, ...), kind=kLoop, calls=%fused_computation.505 | loop fusion | flops 28178432 | bytes 998400 | tf_op jit(solution)/shard_map/reduce_sum | solution.py:71
  90.5 59.8 %all-reduce.5 = (f32[1024]{0:T(1024)S(1)}, f32[1024]{0:T(1024)S(1)}, f32[1024]{0:T(1024)S(1)}, f32[1024]{0:T(1024)S(1)}) all-reduce(f32[1024]{0:T(1024)S(1)} %dynamic-update-slice.2, f32[1024]{0:T(1024)S(1)} %dynamic-update-slice.1, f32[1024]{0:T(1024)S(1)} %get-tuple-element.45, ...), channel_id=1, replica_groups=mesh['mix'=2,'seq'=16] {'seq'}, use_global_device_ids=true, to_apply=%add.2 | all-reduce | flops 4096 | bytes 32768
  150.3 2.5 fusion.293
  152.8 30.0 %all-reduce.4 = (f32[1024]{0:T(1024)S(1)}, f32[1024]{0:T(1024)S(1)}) all-reduce(f32[1024]{0:T(1024)S(1)} %get-tuple-element.43, f32[1024]{0:T(1024)S(1)} %get-tuple-element.42), channel_id=1, replica_groups=mesh['mix'=2,'seq'=16] {'seq'}, use_global_device_ids=true, to_apply=%region_9.0 | all-reduce | flops 2048 | bytes 16384 | tf_op jit(solution)/shard_map/psum | solution.py:101
  182.8 0.9 fusion.250
  183.7 0.3 fusion.162
  184.0 0.4 fusion.208
  184.4 0.7 fusion.247
  185.1 0.7 fusion.180
  185.8 0.7 fusion.198
  186.5 0.2 stack.127
  186.7 1.0 copy.19
  187.7 0.0 reduce-scatter.10.cloned.1.call-update
  187.8 0.0 reduce-scatter.8.cloned.1.call-start
  187.8 2.7 convolution_multiply_fusion.1
  190.6 0.0 reduce-scatter.8.cloned.1.call-update
  190.6 0.2 reduce-scatter.6.cloned.1.call-start
  190.8 1.3 collective-permute-start.4
  192.1 3.0 collective-permute-start.5
  195.2 0.9 collective-permute-done.5
  196.1 4.3 %multiply_convert_fusion.1 = (bf16[128,1024]{1,0:T(8,128)(2,1)S(1)}, f32[128,1024]{1,0:T(8,128)S(1)}) fusion(f32[128,2048]{1,0:T(8,128)S(1)} %fusion.291, f32[128]{0:T(128)S(1)} %get-tuple-element.94, f32[128,1024]{1,0:T(8,128)S(1)} %get-tuple-element.52, f32[15,1024]{1,0:T(8,128)S(1)} %collective-permute-done.5, f32[1024]{0:T(1024)S(1)} %bitcast.108, ...), kind=kLoop, calls=%fused_computation.415 | loop fusion | flops 16515072 | bytes 2100224 | tf_op jit(solution)/shard_map/convert
  200.4 0.2 multiply_convert_fusion
  200.6 4.6 %convolution_multiply_fusion = f32[1024,2048]{1,0:T(8,128)} fusion(bf16[128,1024]{1,0:T(8,128)(2,1)S(1)} %multiply_convert_fusion, bf16[128,1024]{1,0:T(8,128)(2,1)S(1)} %get-tuple-element.53, bf16[128,1024]{1,0:T(8,128)(2,1)S(1)} %copy-done, f32[1024]{0:T(1024)S(1)} %all-reduce, f32[128]{0:T(128)S(1)} %add_rsqrt_fusion.1, f32[128]{0:T(128)S(1)} %broadcast_multiply_fusion.6), kind=kOutput, calls=%fused_computation | convolution fusion | flops 540672000 | bytes 9180160 | tf_op jit(solution)/shard_map/fa,fb->ab/dot_general | solution.py:136
  205.2 0.0 reduce-scatter.6.cloned.1.call-update
  205.9 0.6 dynamic-slice_multiply_fusion
  206.5 3.1 fusion.1
  209.6 1.6 fusion.128
  211.3 31.1 %all-reduce.3 = f32[1024]{0:T(1024)S(1)} all-reduce(f32[1024]{0:T(1024)S(1)} %broadcast_multiply_fusion.1), channel_id=5, replica_groups=mesh['mix'=2,'seq'=16] {'seq'}, use_global_device_ids=true, to_apply=%region_47.0.clone | all-reduce | flops 1024 | bytes 8192
  242.4 0.6 dynamic-slice.4
  243.0 1.0 fusion.127
  244.0 1.4 copy.20
  245.4 72.5 %reduce-scatter.8.cloned.1.call-done = f32[64,1024]{1,0:T(8,128)} async-done(((f32[1024,1024]{1,0:T(8,128)}), f32[64,1024]{1,0:T(8,128)}) %reduce-scatter.8.cloned.1.call-update) | async-done | bytes 262160 | tf_op jit(solution)/shard_map/reduce_scatter | solution.py:87
  317.9 108.2 %reduce-scatter.6.cloned.1.call-done = f32[64,2048]{1,0:T(8,128)} async-done(((f32[1024,2048]{1,0:T(8,128)}), f32[64,2048]{1,0:T(8,128)}) %reduce-scatter.6.cloned.1.call-update) | async-done | bytes 524304 | tf_op jit(solution)/shard_map/reduce_scatter | solution.py:140
  (25 shorter events, 0.1 us)
Async XLA Ops:
  7.2 70.7 %all-gather.4.cloned.1.call-start = ((), (), s32[]{:S(2)}) async-start(), calls=%async_computation.3 | async-start | bytes 4456448 | tf_op jit(solution)/shard_map/all_gather | solution.py:56
  7.9 142.4 %all-gather.6.cloned.1.call-start = ((), (), s32[]{:S(2)}) async-start(), calls=%async_computation.4 | async-start | bytes 2228224 | tf_op jit(solution)/shard_map/all_gather | solution.py:83
  8.6 235.3 %reduce-scatter.10.cloned.1.call-start = ((), (), s32[]{:S(2)}) async-start(), calls=%async_computation.7 | async-start | bytes 557056
  9.4 67.6 %collective-permute-start.1 = (s32[15]{0:T(128)S(1)}, s32[15]{0:T(128)S(1)}, u32[]{:S(2)}, u32[]{:S(2)}) collective-permute-start(s32[15]{0:T(128)S(1)} %get-tuple-element.128), channel_id=1, source_target_pairs={{0,1},{1,2},{2,3},{3,4},{4,5},{5,6},{6,7},{7,8},{8,9},{9,10},{10,1... | collective-permute-start | bytes 188 | tf_op jit(solution)/shard_map/ppermute | solution.py:18
  11.8 65.3 %collective-permute-start.3 = (s32[15]{0:T(128)S(1)}, s32[15]{0:T(128)S(1)}, u32[]{:S(2)}, u32[]{:S(2)}) collective-permute-start(s32[15]{0:T(128)S(1)} %get-tuple-element.129), channel_id=1, source_target_pairs={{1,0},{2,1},{3,2},{4,3},{5,4},{6,5},{7,6},{8,7},{9,8},{10,9},{11,1... | collective-permute-start | bytes 188 | tf_op jit(solution)/shard_map/ppermute | solution.py:20
  39.7 44.3 %copy-start.3 = (s32[128]{0:T(128)S(1)}, s32[128]{0:T(128)}, u32[]{:S(2)}) copy-start(s32[128]{0:T(128)} %param.10) | copy-start | bytes 1540
  76.1 74.2 %copy-start.2 = (bf16[128,1024]{1,0:T(8,128)(2,1)S(1)}, bf16[128,1024]{1,0:T(8,128)(2,1)}, u32[]{:S(2)}) copy-start(bf16[128,1024]{1,0:T(8,128)(2,1)} %param.11) | copy-start | bytes 786436
  81.2 2.9 collective-permute-start
  82.7 3.1 collective-permute-start.2
  187.8 130.1 %reduce-scatter.8.cloned.1.call-start = ((), (), s32[]{:S(2)}) async-start(), calls=%async_computation.6 | async-start | bytes 4456448 | tf_op jit(solution)/shard_map/reduce_scatter | solution.py:87
  190.6 10.0 %copy-start = (bf16[128,1024]{1,0:T(8,128)(2,1)S(1)}, bf16[128,1024]{1,0:T(8,128)(2,1)}, u32[]{:S(2)}) copy-start(bf16[128,1024]{1,0:T(8,128)(2,1)} %param.9) | copy-start | bytes 786436
  190.6 235.5 %reduce-scatter.6.cloned.1.call-start = ((), (), s32[]{:S(2)}) async-start(), calls=%async_computation.5 | async-start | bytes 8912896 | tf_op jit(solution)/shard_map/reduce_scatter | solution.py:140
  190.8 4.3 %collective-permute-start.4 = (f32[15,1024]{1,0:T(8,128)S(1)}, f32[15,1024]{1,0:T(8,128)S(1)}, u32[]{:S(2)}, u32[]{:S(2)}) collective-permute-start(f32[15,1024]{1,0:T(8,128)S(1)} %get-tuple-element.56), channel_id=1, source_target_pairs={{1,0},{2,1},{3,2},{4,3},{5,4},{6,5},{7,6},{8,7},{9,8},{10,9},{11,1... | collective-permute-start | bytes 184328 | tf_op jit(solution)/shard_map/ppermute | solution.py:20
  192.1 3.9 collective-permute-start.5
  205.9 3.7 copy-start.1
Sparse Core Ops, SparseCore 0:
  10.2 54.4 all-gather.3
  66.8 39.9 all-gather.5
  187.9 53.3 reduce-scatter.9
  246.1 71.7 reduce-scatter.7
  322.4 103.6 reduce-scatter.5
where the time goes:
time: 433 us
  waiting for transfers between devices  185 us (43%)
  blocking collectives  178 us (41%)
  other arithmetic  18.4 us (4%)
  matrix products  17.7 us (4%)
  between operations  15.4 us (4%)
  starting transfers between devices  11.1 us (3%)
  local copies, waits for them, and re-layouts  7.65 us (2%)
    unnamed x3, blocking collectives  121 us
    reduce_scatter x1, waiting for transfers between devices, local(): lax.psum_scatter(in_term, 'seq', scatter_dimension=0, tiled=True)  108 us
    reduce_scatter x1, waiting for transfers between devices, local(): lax.psum_scatter(jnp.einsum('fa,fb->ab', activation, out_grad, preferred_...  72.5 us
    psum x1, blocking collectives, local(): lax.psum((jnp.sum(grad_zed, axis=0), jnp.sum(grad_zed * bn_hat, axis=0)),...  30 us
    all_gather x1, blocking collectives, local(): lax.all_gather(dw_kernel, 'seq', axis=1, tiled=True)  26.5 us
  transfers between devices with their start and end apart: 11, of which 4 were waited for; matrix products, arithmetic and copies ran while one was open for 8% of the time, Pallas kernels for 0%

commit v1 on v0

--- a/solution.py
+++ b/solution.py
@@ -5,6 +5,28 @@
 from jax.sharding import PartitionSpec as P
 
 EPSILON = 1e-05
+
+
+def laid_out(parts, dim):
+    shape = list(parts.shape[1:])
+    shape[dim] *= parts.shape[0]
+    return jnp.moveaxis(parts, 0, dim).reshape(shape)
+
+
+def ring_gather(shard, axis, dim):
+    length = lax.axis_size(axis)
+    pairs = [(i, (i + 1) % length) for i in range(length)]
+    back = [(b, a) for a, b in pairs]
+    lower, upper = ([], [])
+    for step in range(length - 1):
+        if step % 2 == 0:
+            lower.append(lax.ppermute(lower[-1] if lower else shard, axis, pairs))
+        else:
+            upper.append(lax.ppermute(upper[-1] if upper else shard, axis, back))
+    blocks = jnp.stack([*lower[::-1], shard, *upper])
+    shift = lax.axis_index(axis) - len(lower)
+    blocks = blocks[(jnp.arange(length) - shift) % length]
+    return laid_out(blocks, dim)
 
 
 def with_halo(cells, sides, width):
@@ -35,7 +57,7 @@
     share = width // devices
     gains, kernel, bn_scale, bn_shift = (
         lax.all_gather(ln_gain, "seq", axis=0, tiled=True),
-        lax.all_gather(dw_kernel, "seq", axis=1, tiled=True),
+        ring_gather(dw_kernel, "seq", 1),
         lax.all_gather(bn_gain, "seq", axis=0, tiled=True),
         lax.all_gather(bn_bias, "seq", axis=0, tiled=True),
     )

time: 433 us -> 455 us (1.051)
  starting transfers between devices: 11.1 us -> 39.3 us
  blocking collectives: 178 us -> 159 us
  waiting for transfers between devices: 185 us -> 192 us
    ppermute x0 -> x15, starting transfers between devices: none -> 29.7 us  [the longest x7 27.5 us: ring_gather(): upper.append(lax.ppermute(upper[-1] if upper else shard, axis, back))]
    all_gather x1 -> x0, blocking collectives: 26.5 us -> none  [local(): lax.all_gather(dw_kernel, 'seq', axis=1, tiled=True)]
    ppermute x0 -> x15, waiting for transfers between devices: none -> 9.73 us  [the longest x8 7.05 us: ring_gather(): lower.append(lax.ppermute(lower[-1] if lower else shard, axis, pairs))]
    unnamed x3, blocking collectives: 121 us -> 129 us
  transfers between devices with their start and end apart: 11 -> 26, of which waited for: 4 -> 12; matrix products, arithmetic and copies ran while one was open for 8% -> 9% of each run, Pallas kernels for 0% -> 0%
where the time goes in v1:
time: 455 us
  waiting for transfers between devices  192 us (42%)
  blocking collectives  159 us (35%)
  starting transfers between devices  39.3 us (9%)
  other arithmetic  19.2 us (4%)
  matrix products  17.8 us (4%)
  between operations  15.5 us (3%)
  local copies, waits for them, and re-layouts  11.5 us (3%)
    unnamed x3, blocking collectives  129 us
    reduce_scatter x1, waiting for transfers between devices, local(): lax.psum_scatter(in_term, 'seq', scatter_dimension=0, tiled=True)  108 us
    reduce_scatter x1, waiting for transfers between devices, local(): lax.psum_scatter(jnp.einsum('fa,fb->ab', activation, out_grad, preferred_...  72.4 us
    psum x1, blocking collectives, local(): lax.psum((jnp.sum(grad_zed, axis=0), jnp.sum(grad_zed * bn_hat, axis=0)),...  30.2 us
    ppermute x7, starting transfers between devices, ring_gather(): upper.append(lax.ppermute(upper[-1] if upper else shard, axis, back))  27.5 us
  transfers between devices with their start and end apart: 26, of which 12 were waited for; matrix products, arithmetic and copies ran while one was open for 9% of the time, Pallas kernels for 0%

profile of v1, /device:TPU:0, one launch (start us, length us, event | category | flops | bytes accessed | tf_op | source)
XLA Modules:
  0.0 454.7 jit_solution(520971405363538209)
XLA Ops:
  7.2 0.7 all-gather.3.cloned.1.call-update
  7.9 0.5 collective-permute-start
  8.4 5.1 %collective-permute-start.8 = (f32[31,64]{1,0:T(8,128)}, f32[31,64]{1,0:T(8,128)S(1)}, u32[]{:S(2)}, u32[]{:S(2)}) collective-permute-start(f32[31,64]{1,0:T(8,128)} %param.14), channel_id=1, source_target_pairs={{1,0},{2,1},{3,2},{4,3},{5,4},{6,5},{7,6},{8,7},{9,8},{10,9},{11,1... | collective-permute-start | bytes 23816 | tf_op jit(solution)/shard_map/ppermute | solution.py:25
  13.5 0.7 broadcast_add_fusion
  14.2 1.3 collective-permute-start.16
  15.5 1.3 collective-permute-start.18
  16.9 1.1 convert_reduce_fusion
  18.0 1.2 collective-permute-start.1
  19.2 1.2 fusion.129
  20.3 3.7 collective-permute-done.1
  24.0 4.4 collective-permute-start.9
  28.5 1.7 collective-permute-done.2
  30.2 4.5 collective-permute-start.10
  34.7 1.5 collective-permute-done.3
  36.2 1.3 fusion.301
  38.2 0.9 dynamic-update-slice.2
  39.0 0.8 dynamic-update-slice
  39.9 0.8 dynamic-update-slice.1
  40.7 34.3 %all-reduce = f32[1024]{0:T(1024)S(1)} all-reduce(f32[1024]{0:T(1024)S(1)} %dynamic-update-slice), channel_id=1, replica_groups=mesh['mix'=2,'seq'=16] {'seq'}, use_global_device_ids=true, to_apply=%add | all-reduce | flops 1024 | bytes 8192
  75.1 0.5 collective-permute-start.5
  75.6 0.9 collective-permute-done.11
  76.5 4.5 collective-permute-start.12
  81.1 0.7 compare_convert_fusion.29
  81.8 0.6 collective-permute-done.12
  82.5 4.5 collective-permute-start.13
  87.0 0.7 compare_convert_fusion.14
  87.7 0.7 collective-permute-done.13
  88.4 4.4 collective-permute-start.14
  93.0 0.7 constant_dynamic-update-slice_fusion.7
  93.8 0.5 collective-permute-done.14
  94.3 0.6 gather_fusion
  94.9 0.4 slice_reduce_fusion.30
  95.3 3.1 fusion.293
  98.6 1.3 collective-permute-start.15
  99.9 1.3 collective-permute-start.17
  101.2 0.3 slice_reduce_fusion.29
  103.7 4.8 %fusion.296 = (f32[1024]{0:T(1024)S(1)}, f32[1024]{0:T(1024)S(1)}, f32[128,1024]{1,0:T(8,128)S(1)}) fusion(f32[128]{0:T(128)S(1)} %get-tuple-element.110, bf16[15,1024]{1,0:T(8,128)(2,1)S(1)} %collective-permute-done.17, bf16[128,1024]{1,0:T(8,128)(2,1)S(1)} %multiply_convert_fusion.3, f32[1024]{0:T(1024)S(1)} %mul.1492, f32[128]{0:T(128)S(1)} %get-tuple-element.111, ...), kind=kLoop, calls=%fused_computation.560 | loop fusion | flops 28178432 | bytes 998400 | tf_op jit(solution)/shard_map/reduce_sum | solution.py:93
  108.5 63.9 %all-reduce.5 = (f32[1024]{0:T(1024)S(1)}, f32[1024]{0:T(1024)S(1)}, f32[1024]{0:T(1024)S(1)}, f32[1024]{0:T(1024)S(1)}) all-reduce(f32[1024]{0:T(1024)S(1)} %dynamic-update-slice.2, f32[1024]{0:T(1024)S(1)} %dynamic-update-slice.1, f32[1024]{0:T(1024)S(1)} %get-tuple-element.45, ...), channel_id=1, replica_groups=mesh['mix'=2,'seq'=16] {'seq'}, use_global_device_ids=true, to_apply=%add.2 | all-reduce | flops 4096 | bytes 32768
  172.4 2.5 fusion.295
  175.0 30.2 %all-reduce.4 = (f32[1024]{0:T(1024)S(1)}, f32[1024]{0:T(1024)S(1)}) all-reduce(f32[1024]{0:T(1024)S(1)} %get-tuple-element.43, f32[1024]{0:T(1024)S(1)} %get-tuple-element.42), channel_id=1, replica_groups=mesh['mix'=2,'seq'=16] {'seq'}, use_global_device_ids=true, to_apply=%region_9.10 | all-reduce | flops 2048 | bytes 16384 | tf_op jit(solution)/shard_map/psum | solution.py:123
  205.2 0.9 fusion.250
  206.1 0.3 fusion.162
  206.4 0.4 fusion.208
  206.7 0.7 fusion.247
  207.5 0.7 fusion.180
  208.2 0.7 fusion.198
  208.8 0.2 stack.195
  209.1 1.0 copy.17
  210.2 2.7 convolution_multiply_fusion.1
  213.0 1.3 collective-permute-start.19
  214.3 3.0 collective-permute-start.20
  217.4 0.9 collective-permute-done.20
  218.2 4.3 multiply_convert_fusion.1
  222.6 0.2 multiply_convert_fusion
  222.8 4.6 %convolution_multiply_fusion = f32[1024,2048]{1,0:T(8,128)} fusion(bf16[128,1024]{1,0:T(8,128)(2,1)S(1)} %multiply_convert_fusion, bf16[128,1024]{1,0:T(8,128)(2,1)S(1)} %get-tuple-element.84, bf16[128,1024]{1,0:T(8,128)(2,1)S(1)} %copy-done, f32[1024]{0:T(1024)S(1)} %all-reduce, f32[128]{0:T(128)S(1)} %add_rsqrt_fusion.1, f32[128]{0:T(128)S(1)} %broadcast_multiply_fusion.6), kind=kOutput, calls=%fused_computation.1 | convolution fusion | flops 540672000 | bytes 9180160 | tf_op jit(solution)/shard_map/fa,fb->ab/dot_general | solution.py:158
  228.0 0.6 dynamic-slice_multiply_fusion
  228.6 3.1 fusion.1
  231.8 1.7 fusion.128
  233.5 31.1 %all-reduce.3 = f32[1024]{0:T(1024)S(1)} all-reduce(f32[1024]{0:T(1024)S(1)} %broadcast_multiply_fusion.1), channel_id=5, replica_groups=mesh['mix'=2,'seq'=16] {'seq'}, use_global_device_ids=true, to_apply=%region_47.48.clone | all-reduce | flops 1024 | bytes 8192
  264.6 0.6 dynamic-slice.4
  265.2 1.0 fusion.127
  266.2 1.4 copy.18
  267.6 72.4 %reduce-scatter.8.cloned.1.call-done = f32[64,1024]{1,0:T(8,128)} async-done(((f32[1024,1024]{1,0:T(8,128)}), f32[64,1024]{1,0:T(8,128)}) %reduce-scatter.8.cloned.1.call-update) | async-done | bytes 262160 | tf_op jit(solution)/shard_map/reduce_scatter | solution.py:109
  340.0 108.1 %reduce-scatter.6.cloned.1.call-done = f32[64,2048]{1,0:T(8,128)} async-done(((f32[1024,2048]{1,0:T(8,128)}), f32[64,2048]{1,0:T(8,128)}) %reduce-scatter.6.cloned.1.call-update) | async-done | bytes 524304 | tf_op jit(solution)/shard_map/reduce_scatter | solution.py:162
  (100 shorter events, 3.2 us)
Async XLA Ops:
  7.2 88.1 %all-gather.3.cloned.1.call-start = ((), (), s32[]{:S(2)}) async-start(), calls=%async_computation.3 | async-start | bytes 4456448 | tf_op jit(solution)/shard_map/all_gather | solution.py:78
  7.9 164.5 %all-gather.5.cloned.1.call-start = ((), (), s32[]{:S(2)}) async-start(), calls=%async_computation.4 | async-start | bytes 2228224 | tf_op jit(solution)/shard_map/all_gather | solution.py:105
  7.9 10.0 %collective-permute-start = (f32[31,64]{1,0:T(8,128)}, f32[31,64]{1,0:T(8,128)S(1)}, u32[]{:S(2)}, u32[]{:S(2)}) collective-permute-start(f32[31,64]{1,0:T(8,128)} %param.14), channel_id=1, source_target_pairs={{0,1},{1,2},{2,3},{3,4},{4,5},{5,6},{6,7},{7,8},{8,9},{9,10},{10,1... | collective-permute-start | bytes 23816 | tf_op jit(solution)/shard_map/ppermute | solution.py:23
  8.4 15.6 %collective-permute-start.8 = (f32[31,64]{1,0:T(8,128)}, f32[31,64]{1,0:T(8,128)S(1)}, u32[]{:S(2)}, u32[]{:S(2)}) collective-permute-start(f32[31,64]{1,0:T(8,128)} %param.14), channel_id=1, source_target_pairs={{1,0},{2,1},{3,2},{4,3},{5,4},{6,5},{7,6},{8,7},{9,8},{10,9},{11,1... | collective-permute-start | bytes 23816 | tf_op jit(solution)/shard_map/ppermute | solution.py:25
  14.2 61.3 %collective-permute-start.16 = (s32[15]{0:T(128)S(1)}, s32[15]{0:T(128)S(1)}, u32[]{:S(2)}, u32[]{:S(2)}) collective-permute-start(s32[15]{0:T(128)S(1)} %get-tuple-element.128), channel_id=1, source_target_pairs={{0,1},{1,2},{2,3},{3,4},{4,5},{5,6},{6,7},{7,8},{8,9},{9,10},{10,1... | collective-permute-start | bytes 188 | tf_op jit(solution)/shard_map/ppermute | solution.py:40
  15.5 60.0 %collective-permute-start.18 = (s32[15]{0:T(128)S(1)}, s32[15]{0:T(128)S(1)}, u32[]{:S(2)}, u32[]{:S(2)}) collective-permute-start(s32[15]{0:T(128)S(1)} %get-tuple-element.129), channel_id=1, source_target_pairs={{1,0},{2,1},{3,2},{4,3},{5,4},{6,5},{7,6},{8,7},{9,8},{10,9},{11,1... | collective-permute-start | bytes 188 | tf_op jit(solution)/shard_map/ppermute | solution.py:42
  16.9 249.3 %reduce-scatter.10.cloned.1.call-start = ((), (), s32[]{:S(2)}) async-start(), calls=%async_computation.7 | async-start | bytes 557056
  18.0 6.0 %collective-permute-start.1 = (f32[31,64]{1,0:T(8,128)S(1)}, f32[31,64]{1,0:T(8,128)S(1)}, u32[]{:S(2)}, u32[]{:S(2)}) collective-permute-start(f32[31,64]{1,0:T(8,128)S(1)} %collective-permute-done), channel_id=1, source_target_pairs={{0,1},{1,2},{2,3},{3,4},{4,5},{5,6},{6,7},{7,8},{8,9},{9,10},{10,1... | collective-permute-start | bytes 23816 | tf_op jit(solution)/shard_map/ppermute | solution.py:23
  24.0 6.1 %collective-permute-start.2 = (f32[31,64]{1,0:T(8,128)S(1)}, f32[31,64]{1,0:T(8,128)S(1)}, u32[]{:S(2)}, u32[]{:S(2)}) collective-permute-start(f32[31,64]{1,0:T(8,128)S(1)} %collective-permute-done.1), channel_id=1, source_target_pairs={{0,1},{1,2},{2,3},{3,4},{4,5},{5,6},{6,7},{7,8},{8,9},{9,10},{10,1... | collective-permute-start | bytes 23816 | tf_op jit(solution)/shard_map/ppermute | solution.py:23
  24.0 6.2 %collective-permute-start.9 = (f32[31,64]{1,0:T(8,128)S(1)}, f32[31,64]{1,0:T(8,128)S(1)}, u32[]{:S(2)}, u32[]{:S(2)}) collective-permute-start(f32[31,64]{1,0:T(8,128)S(1)} %collective-permute-done.8), channel_id=1, source_target_pairs={{1,0},{2,1},{3,2},{4,3},{5,4},{6,5},{7,6},{8,7},{9,8},{10,9},{11,1... | collective-permute-start | bytes 23816 | tf_op jit(solution)/shard_map/ppermute | solution.py:25
  30.2 6.0 %collective-permute-start.3 = (f32[31,64]{1,0:T(8,128)S(1)}, f32[31,64]{1,0:T(8,128)S(1)}, u32[]{:S(2)}, u32[]{:S(2)}) collective-permute-start(f32[31,64]{1,0:T(8,128)S(1)} %collective-permute-done.2), channel_id=1, source_target_pairs={{0,1},{1,2},{2,3},{3,4},{4,5},{5,6},{6,7},{7,8},{8,9},{9,10},{10,1... | collective-permute-start | bytes 23816 | tf_op jit(solution)/shard_map/ppermute | solution.py:23
  30.2 44.8 %collective-permute-start.10 = (f32[31,64]{1,0:T(8,128)S(1)}, f32[31,64]{1,0:T(8,128)S(1)}, u32[]{:S(2)}, u32[]{:S(2)}) collective-permute-start(f32[31,64]{1,0:T(8,128)S(1)} %collective-permute-done.9), channel_id=1, source_target_pairs={{1,0},{2,1},{3,2},{4,3},{5,4},{6,5},{7,6},{8,7},{9,8},{10,9},{11,1... | collective-permute-start | bytes 23816 | tf_op jit(solution)/shard_map/ppermute | solution.py:25
  36.2 38.9 %collective-permute-start.4 = (f32[31,64]{1,0:T(8,128)S(1)}, f32[31,64]{1,0:T(8,128)S(1)}, u32[]{:S(2)}, u32[]{:S(2)}) collective-permute-start(f32[31,64]{1,0:T(8,128)S(1)} %collective-permute-done.3), channel_id=1, source_target_pairs={{0,1},{1,2},{2,3},{3,4},{4,5},{5,6},{6,7},{7,8},{8,9},{9,10},{10,1... | collective-permute-start | bytes 23816 | tf_op jit(solution)/shard_map/ppermute | solution.py:23
  75.0 1.5 collective-permute-start.11
  75.1 6.0 %collective-permute-start.5 = (f32[31,64]{1,0:T(8,128)S(1)}, f32[31,64]{1,0:T(8,128)S(1)}, u32[]{:S(2)}, u32[]{:S(2)}) collective-permute-start(f32[31,64]{1,0:T(8,128)S(1)} %collective-permute-done.4), channel_id=1, source_target_pairs={{0,1},{1,2},{2,3},{3,4},{4,5},{5,6},{6,7},{7,8},{8,9},{9,10},{10,1... | collective-permute-start | bytes 23816 | tf_op jit(solution)/shard_map/ppermute | solution.py:23
  76.5 5.9 %collective-permute-start.12 = (f32[31,64]{1,0:T(8,128)S(1)}, f32[31,64]{1,0:T(8,128)S(1)}, u32[]{:S(2)}, u32[]{:S(2)}) collective-permute-start(f32[31,64]{1,0:T(8,128)S(1)} %collective-permute-done.11), channel_id=1, source_target_pairs={{1,0},{2,1},{3,2},{4,3},{5,4},{6,5},{7,6},{8,7},{9,8},{10,9},{11,1... | collective-permute-start | bytes 23816 | tf_op jit(solution)/shard_map/ppermute | solution.py:25
  81.1 5.9 %collective-permute-start.6 = (f32[31,64]{1,0:T(8,128)S(1)}, f32[31,64]{1,0:T(8,128)S(1)}, u32[]{:S(2)}, u32[]{:S(2)}) collective-permute-start(f32[31,64]{1,0:T(8,128)S(1)} %collective-permute-done.5), channel_id=1, source_target_pairs={{0,1},{1,2},{2,3},{3,4},{4,5},{5,6},{6,7},{7,8},{8,9},{9,10},{10,1... | collective-permute-start | bytes 23816 | tf_op jit(solution)/shard_map/ppermute | solution.py:23
  82.5 6.0 %collective-permute-start.13 = (f32[31,64]{1,0:T(8,128)S(1)}, f32[31,64]{1,0:T(8,128)S(1)}, u32[]{:S(2)}, u32[]{:S(2)}) collective-permute-start(f32[31,64]{1,0:T(8,128)S(1)} %collective-permute-done.12), channel_id=1, source_target_pairs={{1,0},{2,1},{3,2},{4,3},{5,4},{6,5},{7,6},{8,7},{9,8},{10,9},{11,1... | collective-permute-start | bytes 23816 | tf_op jit(solution)/shard_map/ppermute | solution.py:25
  87.0 6.0 %collective-permute-start.7 = (f32[31,64]{1,0:T(8,128)S(1)}, f32[31,64]{1,0:T(8,128)S(1)}, u32[]{:S(2)}, u32[]{:S(2)}) collective-permute-start(f32[31,64]{1,0:T(8,128)S(1)} %collective-permute-done.6), channel_id=1, source_target_pairs={{0,1},{1,2},{2,3},{3,4},{4,5},{5,6},{6,7},{7,8},{8,9},{9,10},{10,1... | collective-permute-start | bytes 23816 | tf_op jit(solution)/shard_map/ppermute | solution.py:23
  88.4 5.9 %collective-permute-start.14 = (f32[31,64]{1,0:T(8,128)S(1)}, f32[31,64]{1,0:T(8,128)S(1)}, u32[]{:S(2)}, u32[]{:S(2)}) collective-permute-start(f32[31,64]{1,0:T(8,128)S(1)} %collective-permute-done.13), channel_id=1, source_target_pairs={{1,0},{2,1},{3,2},{4,3},{5,4},{6,5},{7,6},{8,7},{9,8},{10,9},{11,1... | collective-permute-start | bytes 23816 | tf_op jit(solution)/shard_map/ppermute | solution.py:25
  95.3 77.1 %copy-start.2 = (bf16[128,1024]{1,0:T(8,128)(2,1)S(1)}, bf16[128,1024]{1,0:T(8,128)(2,1)}, u32[]{:S(2)}) copy-start(bf16[128,1024]{1,0:T(8,128)(2,1)} %param.11) | copy-start | bytes 786436
  98.6 5.1 %collective-permute-start.15 = (bf16[15,1024]{1,0:T(8,128)(2,1)S(1)}, bf16[15,1024]{1,0:T(8,128)(2,1)S(1)}, u32[]{:S(2)}, u32[]{:S(2)}) collective-permute-start(bf16[15,1024]{1,0:T(8,128)(2,1)S(1)} %get-tuple-element.89), channel_id=1, source_target_pairs={{0,1},{1,2},{2,3},{3,4},{4,5},{5,6},{6,7},{7,8},{8,9},{9,10},{10,1... | collective-permute-start | bytes 92168 | tf_op jit(solution)/shard_map/ppermute | solution.py:40
  99.9 3.8 collective-permute-start.17
  210.1 129.9 %reduce-scatter.8.cloned.1.call-start = ((), (), s32[]{:S(2)}) async-start(), calls=%async_computation.6 | async-start | bytes 4456448 | tf_op jit(solution)/shard_map/reduce_scatter | solution.py:109
  212.9 9.8 %copy-start = (bf16[128,1024]{1,0:T(8,128)(2,1)S(1)}, bf16[128,1024]{1,0:T(8,128)(2,1)}, u32[]{:S(2)}) copy-start(bf16[128,1024]{1,0:T(8,128)(2,1)} %param.9) | copy-start | bytes 786436
  212.9 235.2 %reduce-scatter.6.cloned.1.call-start = ((), (), s32[]{:S(2)}) async-start(), calls=%async_computation.5 | async-start | bytes 8912896 | tf_op jit(solution)/shard_map/reduce_scatter | solution.py:162
  213.0 4.3 collective-permute-start.19
  214.3 3.9 collective-permute-start.20
  228.0 3.7 copy-start.1
Sparse Core Ops, SparseCore 0:
  10.2 53.9 all-gather.2
  66.4 40.2 all-gather.4
  210.2 53.1 reduce-scatter.9
  268.2 71.7 reduce-scatter.7
  344.5 103.5 reduce-scatter.5
